TPU v7x, 128 devices: a whole 4x4x4 slice. The times are simulated.
128 devices in a mesh: expert: 16 (over y, x), etp: 8 (over z, core).
Axes of the slice: x: 4, y: 4, z: 4, core: 2. Of those that a mesh axis runs over, the one named last changes fastest.
Arguments:
- tokens: bfloat16 [2048, 2048], P('expert'), may hold values from -6 to 6
- out_grad: bfloat16 [2048, 2048], P('expert'), may hold values from -6 to 6
- routes: int32 [2048, 2], P('expert'), may hold values from 0 to 15, as said below
- combine_weights: float32 [2048, 2], P('expert'), may hold values from 0.2 to 1
- w_gate: bfloat16 [16, 2048, 7168], P('expert', None, 'etp'), may hold values from -0.125 to 0.125
- w_up: bfloat16 [16, 2048, 7168], P('expert', None, 'etp'), may hold values from -0.125 to 0.125
- w_down: bfloat16 [16, 7168, 2048], P('expert', 'etp'), may hold values from -0.0625 to 0.0625
Outputs:
- mixed: bfloat16 [2048, 2048], P('expert')
- tokens_grad: bfloat16 [2048, 2048], P('expert')
- combine_grad: float32 [2048, 2], P('expert')
- gate_weight_grad: bfloat16 [16, 2048, 7168], P('expert', None, 'etp')
- up_weight_grad: bfloat16 [16, 2048, 7168], P('expert', None, 'etp')
- down_weight_grad: bfloat16 [16, 7168, 2048], P('expert', 'etp')
Inputs may be any that keep to these rules, and one draw needn't show every extreme that they name: `routes`: each token names two different experts. No expert is named by more than 32 tokens of one group of 128 consecutive tokens, and one expert, the same in every group, is named by exactly 32 tokens of each group.
All inputs are finite; a program needn't handle non-finite values.
Results may differ from a plain program's by a relative error of at most 0.02.
Values may be sent and summed in bfloat16 or wider, within the bound.
No kernel may reach another device: no remote copies, remote signals or barrier semaphores. Data moves between devices by JAX's collectives and lax.ppermute only.
A program may use at most 128 MiB of HBM per device.

v0:
```python
import jax
import jax.numpy as jnp
from jax import lax
from jax.sharding import PartitionSpec as P

TOP = 2


def slot_numbers(routes, expert_count):
    flattened = routes.reshape(-1)
    one_hot = (flattened[:, None] == jnp.arange(expert_count, dtype=jnp.int32)[None, :]).astype(
        jnp.int32
    )
    before = jnp.cumsum(one_hot, axis=0) - one_hot
    return jnp.sum(before * one_hot, axis=1).reshape(routes.shape)


def contract_last(left, right):
    return lax.dot_general(
        left, right, (((1,), (1,)), ((), ())), preferred_element_type=jnp.float32
    )


def contract_first(left, right):
    return lax.dot_general(
        left, right, (((0,), (0,)), ((), ())), preferred_element_type=jnp.float32
    )


def expert_pass(rows_in, rows_grad, gate_w, up_w, down_w):
    gate_pre = jnp.dot(rows_in, gate_w, preferred_element_type=jnp.float32)
    up_pre = jnp.dot(rows_in, up_w, preferred_element_type=jnp.float32)
    gate_sig = jax.nn.sigmoid(gate_pre)
    swish = gate_pre * gate_sig
    hidden = (swish * up_pre).astype(jnp.bfloat16)
    out_part = jnp.dot(hidden, down_w, preferred_element_type=jnp.float32)
    hidden_grad = contract_last(rows_grad, down_w)
    down_grad = contract_first(hidden, rows_grad).astype(jnp.bfloat16)
    gate_grad = (hidden_grad * up_pre * gate_sig * (1.0 + gate_pre * (1.0 - gate_sig))).astype(
        jnp.bfloat16
    )
    up_grad = (hidden_grad * swish).astype(jnp.bfloat16)
    gate_weight_grad = contract_first(rows_in, gate_grad).astype(jnp.bfloat16)
    up_weight_grad = contract_first(rows_in, up_grad).astype(jnp.bfloat16)
    input_part = contract_last(gate_grad, gate_w) + contract_last(up_grad, up_w)
    return (out_part, input_part, gate_weight_grad, up_weight_grad, down_grad)


def shards(tokens, out_grad, routes, combine_weights, w_gate, w_up, w_down):
    expert_count = lax.axis_size("expert")
    token_count, features = tokens.shape
    capacity = token_count // 4
    slots = slot_numbers(routes, expert_count)
    position = routes * capacity + slots
    pair_count = token_count * TOP
    source_index = jnp.full((expert_count * capacity,), pair_count, jnp.int32)
    source_index = source_index.at[position.reshape(-1)].set(
        jnp.arange(pair_count, dtype=jnp.int32)
    )
    zero_row = jnp.zeros((1, features), jnp.bfloat16)
    padded_tokens = jnp.concatenate([tokens, zero_row], axis=0)
    scaled_grad = (combine_weights[:, :, None] * out_grad[:, None, :]).astype(jnp.bfloat16)
    padded_grad = jnp.concatenate([scaled_grad.reshape(pair_count, features), zero_row], axis=0)
    send_rows = padded_tokens[source_index // TOP].reshape(expert_count, capacity, features)
    send_grad = padded_grad[source_index].reshape(expert_count, capacity, features)
    recv_rows, recv_grad = (
        lax.all_to_all(send_rows, "expert", split_axis=0, concat_axis=0, tiled=True),
        lax.all_to_all(send_grad, "expert", split_axis=0, concat_axis=0, tiled=True),
    )
    rows_in = recv_rows.reshape(expert_count * capacity, features)
    rows_grad = recv_grad.reshape(expert_count * capacity, features)
    out_part, input_part, gate_weight_grad, up_weight_grad, down_weight_grad = expert_pass(
        rows_in, rows_grad, w_gate[0], w_up[0], w_down[0]
    )
    out_part = out_part.reshape(expert_count, capacity, features)
    input_part = input_part.reshape(expert_count, capacity, features)
    grad_values = out_grad.astype(jnp.float32)
    out_sum, input_sum = (
        lax.psum(out_part.astype(jnp.bfloat16), "etp").astype(jnp.float32),
        lax.psum(input_part.astype(jnp.bfloat16), "etp").astype(jnp.float32),
    )
    out_back, input_back = (
        lax.all_to_all(
            out_sum.astype(jnp.bfloat16), "expert", split_axis=0, concat_axis=0, tiled=True
        ),
        lax.all_to_all(
            input_sum.astype(jnp.bfloat16), "expert", split_axis=0, concat_axis=0, tiled=True
        ),
    )
    out_pairs = out_back.reshape(expert_count * capacity, features)[position].astype(jnp.float32)
    input_pairs = input_back.reshape(expert_count * capacity, features)[position].astype(
        jnp.float32
    )
    mixed = jnp.sum(combine_weights[:, :, None] * out_pairs, axis=1).astype(jnp.bfloat16)
    combine_grad = jnp.sum(grad_values[:, None, :] * out_pairs, axis=2)
    tokens_grad = jnp.sum(input_pairs, axis=1).astype(jnp.bfloat16)
    return (
        mixed,
        tokens_grad,
        combine_grad,
        gate_weight_grad[None],
        up_weight_grad[None],
        down_weight_grad[None],
    )


def solution(mesh):
    return jax.shard_map(
        shards,
        mesh=mesh,
        in_specs=(
            P("expert", None),
            P("expert", None),
            P("expert", None),
            P("expert", None),
            P("expert", None, "etp"),
            P("expert", None, "etp"),
            P("expert", "etp", None),
        ),
        out_specs=(
            P("expert", None),
            P("expert", None),
            P("expert", None),
            P("expert", None, "etp"),
            P("expert", None, "etp"),
            P("expert", "etp", None),
        ),
        check_vma=False,
    )
```

profile of v0, /device:TPU:1, one launch (start us, length us, event | category | flops | bytes accessed | tf_op | source)
XLA Modules:
  0.0 260.7 jit_solution(16705591363725790153)
XLA Ops:
  12.9 3.3 %gather_fusion = bf16[512,2048]{1,0:T(8,128)(2,1)} fusion(bf16[129,2048]{1,0:T(8,128)(2,1)S(1)} %concatenate.6, s32[1024]{0:T(1024)S(1)} %get-tuple-element.30), kind=kCustom, calls=%fused_computation | custom fusion | bytes 4196352 | tf_op jit(solution)/shard_map/gather | solution.py:64
  16.2 7.8 %all-to-all-start = ((bf16[16,32,2048]{2,1,0:T(8,128)(2,1)}), bf16[16,32,2048]{2,1,0:T(8,128)(2,1)}, u32[]{:S(2)}, u32[]{:S(2)}) async-start(bf16[16,32,2048]{2,1,0:T(8,128)(2,1)} %bitcast.2), calls=%async_computation | async-start | bytes 4194304 | tf_op jit(solution)/shard_map/all_to_all | solution.py:67
  25.3 2.4 mul.72
  27.7 1.8 multiply_convert_fusion
  29.6 3.3 %gather_fusion.2 = bf16[512,2048]{1,0:T(8,128)(2,1)} fusion(bf16[257,2048]{1,0:T(8,128)(2,1)S(1)} %concatenate.7, s32[1024]{0:T(1024)S(1)} %get-tuple-element.29), kind=kCustom, calls=%fused_computation.2 | custom fusion | bytes 4196352 | tf_op jit(solution)/shard_map/gather | solution.py:65
  32.9 21.6 %all-to-all-done = bf16[16,32,2048]{2,1,0:T(8,128)(2,1)} async-done(((bf16[16,32,2048]{2,1,0:T(8,128)(2,1)}), bf16[16,32,2048]{2,1,0:T(8,128)(2,1)}, u32[]{:S(2)}, u32[]{:S(2)}) %all-to-all-start) | async-done | bytes 2097184 | tf_op jit(solution)/shard_map/all_to_all | solution.py:67
  54.5 4.3 %all-to-all-start.2 = ((bf16[16,32,2048]{2,1,0:T(8,128)(2,1)}), bf16[16,32,2048]{2,1,0:T(8,128)(2,1)S(1)}, u32[]{:S(2)}, u32[]{:S(2)}) async-start(bf16[16,32,2048]{2,1,0:T(8,128)(2,1)} %bitcast.10), calls=%async_computation.2 | async-start | bytes 4194304 | tf_op jit(solution)/shard_map/all_to_all | solution.py:68
  59.0 6.2 %fusion.6 = f32[512,896]{1,0:T(8,128)} fusion(bf16[512,2048]{1,0:T(8,128)(2,1)} %bitcast.3, bf16[1,2048,896]{2,1,0:T(8,128)(2,1)} %param.12), kind=kOutput, calls=%fused_computation.12 | convolution fusion | flops 1879048192 | bytes 7602176 | tf_op jit(solution)/shard_map/dot_general | solution.py:32
  65.2 22.3 %all-to-all-done.2 = bf16[16,32,2048]{2,1,0:T(8,128)(2,1)S(1)} async-done(((bf16[16,32,2048]{2,1,0:T(8,128)(2,1)}), bf16[16,32,2048]{2,1,0:T(8,128)(2,1)S(1)}, u32[]{:S(2)}, u32[]{:S(2)}) %all-to-all-start.2) | async-done | bytes 2097184 | tf_op jit(solution)/shard_map/all_to_all | solution.py:68
  87.5 5.2 %fusion.2 = f32[512,896]{1,0:T(8,128)S(1)} fusion(bf16[512,2048]{1,0:T(8,128)(2,1)S(1)} %bitcast.70, bf16[1,896,2048]{2,1,0:T(8,128)(2,1)} %param.13), kind=kOutput, calls=%fused_computation.8 | convolution fusion | flops 1879048192 | bytes 7602176 | tf_op jit(solution)/shard_map/dot_general | solution.py:19
  92.8 4.8 %multiply_convert_fusion.2 = (bf16[512,896]{1,0:T(8,128)(2,1)S(1)}, bf16[512,896]{1,0:T(8,128)(2,1)S(1)}, bf16[512,896]{1,0:T(8,128)(2,1)S(1)}) fusion(f32[512,896]{1,0:T(8,128)S(1)} %fusion.2, f32[512,896]{1,0:T(8,128)S(1)} %copy-done.12, bf16[512,2048]{1,0:T(8,128)(2,1)} %bitcast.3, bf16[1,2048,896]{2,1,0:T(8,128)(2,1)S(1)} %copy-done.6), kind=kOutput, calls=%fused_computation.26 | convolution fusion | flops 1885929472 | bytes 12189696 | tf_op jit(solution)/shard_map/dot_general | solution.py:31
  97.6 2.4 fusion.4
  100.6 3.7 %fusion.12 = bf16[16,32,2048]{2,1,0:T(8,128)(2,1)} fusion(bf16[16,32,896]{2,1,0:T(8,128)(2,1)S(1)} %bitcast.74, bf16[1,896,2048]{2,1,0:T(8,128)(2,1)S(1)} %copy-done.5), kind=kOutput, calls=%fused_computation.21 | convolution fusion | flops 1880096768 | bytes 6684672 | tf_op jit(solution)/shard_map/dot_general | solution.py:36
  104.3 3.7 %add_convert_fusion = bf16[512,2048]{1,0:T(8,128)(2,1)} fusion(f32[512,2048]{1,0:T(8,128)S(1)} %fusion.4, bf16[512,896]{1,0:T(8,128)(2,1)S(1)} %get-tuple-element.24, bf16[1,2048,896]{2,1,0:T(8,128)(2,1)S(1)} %copy-done.6), kind=kOutput, calls=%fused_computation.5 | convolution fusion | flops 1881145344 | bytes 10878976 | tf_op jit(solution)/shard_map/dot_general | solution.py:19
  108.0 72.5 %all-reduce.5.cloned.1.call-done = (bf16[16,32,2048]{2,1,0:T(8,128)(2,1)}, bf16[16,32,2048]{2,1,0:T(8,128)(2,1)}) async-done(((bf16[16,32,2048]{2,1,0:T(8,128)(2,1)}, bf16[16,32,2048]{2,1,0:T(8,128)(2,1)}), (bf16[16,32,2048]{2,1,0:T(8,128)(2,1)}, bf16[16,32,2048]{2,1,0:T(8,128)(2,1)})) %all-reduce.5.cloned.1.call-update) | async-done | bytes 4194320 | tf_op jit(solution)/shard_map/psum | solution.py:79
  180.4 32.6 %all_to_all.20 = bf16[16,32,2048]{2,1,0:T(8,128)(2,1)} all-to-all(bf16[16,32,2048]{2,1,0:T(8,128)(2,1)} %get-tuple-element.20), channel_id=1, replica_groups=mesh['expert'=16,'etp'=8] {'expert'}, dimensions={0} | all-to-all | bytes 4194304 | tf_op jit(solution)/shard_map/all_to_all | solution.py:83
  213.0 3.9 %all-to-all-start.3 = ((bf16[16,32,2048]{2,1,0:T(8,128)(2,1)}), bf16[16,32,2048]{2,1,0:T(8,128)(2,1)S(1)}, u32[]{:S(2)}, u32[]{:S(2)}) async-start(bf16[16,32,2048]{2,1,0:T(8,128)(2,1)} %get-tuple-element.21), calls=%async_computation.3 | async-start | bytes 4194304 | tf_op jit(solution)/shard_map/all_to_all | solution.py:86
  218.4 6.1 %convert_bitcast_fusion.1 = bf16[1,2048,896]{2,1,0:T(8,128)(2,1)} fusion(bf16[512,2048]{1,0:T(8,128)(2,1)} %bitcast.3, bf16[512,896]{1,0:T(8,128)(2,1)} %copy-done.9), kind=kOutput, calls=%fused_computation.19 | convolution fusion | flops 1880883200 | bytes 6684672 | tf_op jit(solution)/shard_map/dot_general | solution.py:25
  224.5 6.0 %convert_bitcast_fusion.2 = bf16[1,2048,896]{2,1,0:T(8,128)(2,1)} fusion(bf16[512,2048]{1,0:T(8,128)(2,1)} %bitcast.3, bf16[512,896]{1,0:T(8,128)(2,1)S(1)} %copy-done.11), kind=kOutput, calls=%fused_computation.20 | convolution fusion | flops 1880883200 | bytes 6684672 | tf_op jit(solution)/shard_map/dot_general | solution.py:25
  230.5 4.0 %convert_bitcast_fusion = bf16[1,896,2048]{2,1,0:T(8,128)(2,1)} fusion(bf16[512,896]{1,0:T(8,128)(2,1)S(1)} %copy-done.8, bf16[512,2048]{1,0:T(8,128)(2,1)S(1)} %bitcast.71), kind=kOutput, calls=%fused_computation.18 | convolution fusion | flops 1880883200 | bytes 6684672 | tf_op jit(solution)/shard_map/dot_general | solution.py:25
  234.4 4.2 %gather_fusion.1 = bf16[256,2048]{1,0:T(8,128)(2,1)S(1)} fusion(bf16[512,2048]{1,0:T(8,128)(2,1)} %bitcast.69, s32[1024]{0:T(1024)S(1)} %pad_clamp_fusion.1), kind=kCustom, calls=%fused_computation.1 | custom fusion | bytes 2098176 | tf_op jit(solution)/shard_map/gather | solution.py:90
  238.7 2.3 reshape.147
  241.0 6.5 %multiply_reduce_fusion = (f32[128,2]{1,0:T(8,128)S(1)}, bf16[128,2048]{1,0:T(8,128)(2,1)}) fusion(f32[128,2,2048]{2,1,0:T(2,128)} %reshape.147, f32[128,2048]{1,0:T(8,128)} %convert_element_type.61, f32[128,2]{1,0:T(8,128)S(1)} %copy.29), kind=kLoop, calls=%fused_computation.22 | loop fusion | flops 1834752 | bytes 3672064 | tf_op jit(solution)/shard_map/reduce_sum | solution.py:95
  250.3 3.6 %reduce_sum.41 = bf16[128,2048]{1,0:T(8,128)(2,1)} reduce(bf16[128,2,2048]{2,1,0:T(2,128)(2,1)S(1)} %reshape.130, bf16[]{:T(256)} %constant.12.clone.1), dimensions={1}, to_apply=%region_7.8 | reduce | flops 262144 | bytes 1572866 | tf_op jit(solution)/shard_map/reduce_sum | solution.py:96
  (60 shorter events, 12.1 us)
Async XLA Ops:
  16.2 7.8 %copy-start.3 = (f32[128,2]{0,1:T(2,128)S(1)}, f32[128,2]{0,1:T(2,128)}, u32[]{:S(2)}) copy-start(f32[128,2]{0,1:T(2,128)} %param.10) | copy-start | bytes 3076
  16.2 8.0 %copy-start = (bf16[128,2048]{1,0:T(8,128)(2,1)S(1)}, bf16[128,2048]{1,0:T(8,128)(2,1)}, u32[]{:S(2)}) copy-start(bf16[128,2048]{1,0:T(8,128)(2,1)} %param.8) | copy-start | bytes 1572868
  16.2 38.3 %all-to-all-start = ((bf16[16,32,2048]{2,1,0:T(8,128)(2,1)}), bf16[16,32,2048]{2,1,0:T(8,128)(2,1)}, u32[]{:S(2)}, u32[]{:S(2)}) async-start(bf16[16,32,2048]{2,1,0:T(8,128)(2,1)} %bitcast.2), calls=%async_computation | async-start | bytes 4194304 | tf_op jit(solution)/shard_map/all_to_all | solution.py:67
  54.5 33.0 %all-to-all-start.2 = ((bf16[16,32,2048]{2,1,0:T(8,128)(2,1)}), bf16[16,32,2048]{2,1,0:T(8,128)(2,1)S(1)}, u32[]{:S(2)}, u32[]{:S(2)}) async-start(bf16[16,32,2048]{2,1,0:T(8,128)(2,1)} %bitcast.10), calls=%async_computation.2 | async-start | bytes 4194304 | tf_op jit(solution)/shard_map/all_to_all | solution.py:68
  58.8 121.6 %all-reduce.5.cloned.1.call-start = ((), (), s32[]{:S(2)}) async-start(), calls=%async_computation.4 | async-start | bytes 8388608 | tf_op jit(solution)/shard_map/psum | solution.py:79
  87.5 5.2 %copy-start.1 = (bf16[16,32,2048]{2,1,0:T(8,128)(2,1)}, bf16[16,32,2048]{2,1,0:T(8,128)(2,1)S(1)}, u32[]{:S(2)}) copy-start(bf16[16,32,2048]{2,1,0:T(8,128)(2,1)S(1)} %all-to-all-done.2) | copy-start | bytes 6291460
  87.5 5.2 %copy-start.6 = (bf16[1,2048,896]{2,1,0:T(8,128)(2,1)S(1)}, bf16[1,2048,896]{2,1,0:T(8,128)(2,1)}, u32[]{:S(2)}) copy-start(bf16[1,2048,896]{2,1,0:T(8,128)(2,1)} %param.11) | copy-start | bytes 11010052
  87.5 5.2 %copy-start.12 = (f32[512,896]{1,0:T(8,128)S(1)}, f32[512,896]{1,0:T(8,128)}, u32[]{:S(2)}) copy-start(f32[512,896]{1,0:T(8,128)} %fusion.6) | copy-start | bytes 5505028
  92.8 4.8 %copy-start.4 = (bf16[1,2048,896]{2,1,0:T(8,128)(2,1)S(1)}, bf16[1,2048,896]{2,1,0:T(8,128)(2,1)}, u32[]{:S(2)}) copy-start(bf16[1,2048,896]{2,1,0:T(8,128)(2,1)} %param.12) | copy-start | bytes 11010052
  97.5 2.4 copy-start.9
  97.6 2.4 copy-start.7
  97.6 6.7 %copy-start.10 = (bf16[512,896]{1,0:T(8,128)(2,1)}, bf16[512,896]{1,0:T(8,128)(2,1)S(1)}, u32[]{:S(2)}) copy-start(bf16[512,896]{1,0:T(8,128)(2,1)S(1)} %get-tuple-element.24) | copy-start | bytes 2752516
  97.6 3.0 %copy-start.5 = (bf16[1,896,2048]{2,1,0:T(8,128)(2,1)S(1)}, bf16[1,896,2048]{2,1,0:T(8,128)(2,1)}, u32[]{:S(2)}) copy-start(bf16[1,896,2048]{2,1,0:T(8,128)(2,1)} %param.13) | copy-start | bytes 11010052
  213.0 35.2 %all-to-all-start.3 = ((bf16[16,32,2048]{2,1,0:T(8,128)(2,1)}), bf16[16,32,2048]{2,1,0:T(8,128)(2,1)S(1)}, u32[]{:S(2)}, u32[]{:S(2)}) async-start(bf16[16,32,2048]{2,1,0:T(8,128)(2,1)} %get-tuple-element.21), calls=%async_computation.3 | async-start | bytes 4194304 | tf_op jit(solution)/shard_map/all_to_all | solution.py:86
  218.4 6.1 %copy-start.11 = (bf16[512,896]{1,0:T(8,128)(2,1)S(1)}, bf16[512,896]{1,0:T(8,128)(2,1)}, u32[]{:S(2)}) copy-start(bf16[512,896]{1,0:T(8,128)(2,1)} %copy-done.10) | copy-start | bytes 2752516
  224.5 6.0 %copy-start.2 = (bf16[16,32,2048]{2,1,0:T(8,128)(2,1)S(1)}, bf16[16,32,2048]{2,1,0:T(8,128)(2,1)}, u32[]{:S(2)}) copy-start(bf16[16,32,2048]{2,1,0:T(8,128)(2,1)} %copy-done.1) | copy-start | bytes 6291460
  224.5 6.0 %copy-start.8 = (bf16[512,896]{1,0:T(8,128)(2,1)S(1)}, bf16[512,896]{1,0:T(8,128)(2,1)}, u32[]{:S(2)}) copy-start(bf16[512,896]{1,0:T(8,128)(2,1)} %copy-done.7) | copy-start | bytes 2752516
Sparse Core Ops, SparseCore 0:
  108.1 72.2 all-reduce.4
where the time goes:
time: 265 us; the launch traced here: 261 us
  waiting for transfers between devices  116 us (44%)
  matrix products  42 us (16%)
  blocking collectives  32.6 us (12%)
  local copies, waits for them, and re-layouts  24.8 us (9%)
  starting transfers between devices  16.2 us (6%)
  other arithmetic  14.5 us (5%)
  between operations  14.3 us (5%)
    psum x1, waiting for transfers between devices, shards(): lax.psum(out_part.astype(jnp.bfloat16), 'etp').astype(jnp.float32)  72.5 us
    all_to_all x1, blocking collectives, shards(): lax.all_to_all(out_sum.astype(jnp.bfloat16), 'expert', split_axis=0, conc...  32.6 us
    all_to_all x1, waiting for transfers between devices, shards(): lax.all_to_all(send_grad, 'expert', split_axis=0, concat_axis=0, tiled=True)  22.3 us
    all_to_all x1, waiting for transfers between devices, shards(): lax.all_to_all(send_rows, 'expert', split_axis=0, concat_axis=0, tiled=True)  21.6 us
    dot_general x3, matrix products, contract_first(): lax.dot_general(left, right, (((0,), (0,)), ((), ())), preferred_element_...  16 us
    dot_general x3, matrix products, contract_last(): lax.dot_general(left, right, (((1,), (1,)), ((), ())), preferred_element_...  11.3 us
    all_to_all x1, starting transfers between devices, shards(): lax.all_to_all(send_rows, 'expert', split_axis=0, concat_axis=0, tiled=True)  7.77 us
    reduce_sum x1, other arithmetic, shards(): combine_grad = jnp.sum(grad_values[:, None, :] * out_pairs, axis=2)  6.54 us
  transfers between devices with their start and end apart: 4, of which 3 were waited for; matrix products, arithmetic and copies ran while one was open for 18% of the time, Pallas kernels for 0%

commit v1 on v0

v1 whole, which is shorter than its diff:
```python
import jax
import jax.numpy as jnp
from jax import lax
from jax.sharding import PartitionSpec as P

TOP = 2


def contract_last(left, right):
    return lax.dot_general(
        left, right, (((1,), (1,)), ((), ())), preferred_element_type=jnp.float32
    )


def contract_first(left, right):
    return lax.dot_general(
        left, right, (((0,), (0,)), ((), ())), preferred_element_type=jnp.float32
    )


def select_rows(selector, table):
    return jnp.dot(selector.astype(table.dtype), table, preferred_element_type=jnp.float32)


def expert_pass(rows_in, rows_grad, gate_w, up_w, down_w):
    gate_pre = jnp.dot(rows_in, gate_w, preferred_element_type=jnp.float32)
    up_pre = jnp.dot(rows_in, up_w, preferred_element_type=jnp.float32)
    gate_sig = jax.nn.sigmoid(gate_pre)
    swish = gate_pre * gate_sig
    hidden = (swish * up_pre).astype(jnp.bfloat16)
    out_part = jnp.dot(hidden, down_w, preferred_element_type=jnp.float32)
    hidden_grad = contract_last(rows_grad, down_w)
    down_grad = contract_first(hidden, rows_grad).astype(jnp.bfloat16)
    gate_grad = (hidden_grad * up_pre * gate_sig * (1.0 + gate_pre * (1.0 - gate_sig))).astype(
        jnp.bfloat16
    )
    up_grad = (hidden_grad * swish).astype(jnp.bfloat16)
    gate_weight_grad = contract_first(rows_in, gate_grad).astype(jnp.bfloat16)
    up_weight_grad = contract_first(rows_in, up_grad).astype(jnp.bfloat16)
    input_part = contract_last(gate_grad, gate_w) + contract_last(up_grad, up_w)
    return (out_part, input_part, gate_weight_grad, up_weight_grad, down_grad)


def shards(tokens, out_grad, routes, combine_weights, w_gate, w_up, w_down):
    expert_count = lax.axis_size("expert")
    split_count = lax.axis_size("etp")
    me = lax.axis_index("etp")
    token_count, features = tokens.shape
    capacity = token_count // 4
    per_split = capacity // split_count
    pair_count = token_count * TOP

    flat_routes = routes.reshape(pair_count)
    expert_hot = (flat_routes[:, None] == jnp.arange(expert_count, dtype=jnp.int32)[None, :]).astype(
        jnp.int32
    )
    before = jnp.cumsum(expert_hot, axis=0) - expert_hot
    slots = jnp.sum(before * expert_hot, axis=1)

    mine = (slots // per_split) == me
    local_place = jnp.where(mine, flat_routes * per_split + slots % per_split, -1)
    place_count = expert_count * per_split
    pick = local_place[None, :] == jnp.arange(place_count, dtype=jnp.int32)[:, None]
    pick_tokens = jnp.any(pick.reshape(place_count, token_count, TOP), axis=2)

    scaled_grad = (combine_weights[:, :, None] * out_grad.astype(jnp.float32)[:, None, :]).astype(
        jnp.bfloat16
    )
    send_rows = select_rows(pick_tokens, tokens).astype(jnp.bfloat16)
    send_grad = select_rows(pick, scaled_grad.reshape(pair_count, features)).astype(jnp.bfloat16)
    send = jnp.concatenate(
        [
            send_rows.reshape(expert_count, per_split, features),
            send_grad.reshape(expert_count, per_split, features),
        ],
        axis=1,
    )
    recv = lax.all_to_all(send, "expert", split_axis=0, concat_axis=0, tiled=True)
    rows_in = lax.all_gather(recv[:, :per_split], "etp", axis=0, tiled=False).reshape(
        split_count * expert_count * per_split, features
    )
    rows_grad = lax.all_gather(recv[:, per_split:], "etp", axis=0, tiled=False).reshape(
        split_count * expert_count * per_split, features
    )

    out_part, input_part, gate_weight_grad, up_weight_grad, down_weight_grad = expert_pass(
        rows_in, rows_grad, w_gate[0], w_up[0], w_down[0]
    )
    out_sum = lax.psum_scatter(out_part.astype(jnp.bfloat16), "etp", scatter_dimension=0, tiled=True)
    input_sum = lax.psum_scatter(
        input_part.astype(jnp.bfloat16), "etp", scatter_dimension=0, tiled=True
    )
    back = jnp.concatenate(
        [
            out_sum.reshape(expert_count, per_split, features),
            input_sum.reshape(expert_count, per_split, features),
        ],
        axis=1,
    )
    back = lax.all_to_all(back, "expert", split_axis=0, concat_axis=0, tiled=True)
    out_table = back[:, :per_split].reshape(place_count, features)
    input_table = back[:, per_split:].reshape(place_count, features)

    gather = pick.T
    out_pairs = select_rows(gather, out_table).reshape(token_count, TOP, features)
    input_pairs = select_rows(gather, input_table).reshape(token_count, TOP, features)
    grad_values = out_grad.astype(jnp.float32)
    mixed_part = jnp.sum(combine_weights[:, :, None] * out_pairs, axis=1)
    tokens_part = jnp.sum(input_pairs, axis=1)
    combine_part = jnp.sum(grad_values[:, None, :] * out_pairs, axis=2)
    combine_high = combine_part.astype(jnp.bfloat16)
    combine_low = (combine_part - combine_high.astype(jnp.float32)).astype(jnp.bfloat16)
    pad = jnp.zeros((token_count, 128 - 2 * TOP), jnp.bfloat16)
    packed = jnp.concatenate(
        [
            mixed_part.astype(jnp.bfloat16),
            tokens_part.astype(jnp.bfloat16),
            combine_high,
            combine_low,
            pad,
        ],
        axis=1,
    )
    total = lax.psum(packed, "etp")
    mixed = total[:, :features]
    tokens_grad = total[:, features : 2 * features]
    combine_grad = total[:, 2 * features : 2 * features + TOP].astype(jnp.float32) + total[
        :, 2 * features + TOP : 2 * features + 2 * TOP
    ].astype(jnp.float32)
    return (
        mixed,
        tokens_grad,
        combine_grad,
        gate_weight_grad[None],
        up_weight_grad[None],
        down_weight_grad[None],
    )


def solution(mesh):
    return jax.shard_map(
        shards,
        mesh=mesh,
        in_specs=(
            P("expert", None),
            P("expert", None),
            P("expert", None),
            P("expert", None),
            P("expert", None, "etp"),
            P("expert", None, "etp"),
            P("expert", "etp", None),
        ),
        out_specs=(
            P("expert", None),
            P("expert", None),
            P("expert", None),
            P("expert", None, "etp"),
            P("expert", None, "etp"),
            P("expert", "etp", None),
        ),
        check_vma=False,
    )
```

time: 265 us -> 279 us (1.053)
  waiting for transfers between devices: 116 us -> 160 us
  blocking collectives: 32.6 us -> 17.9 us
  other arithmetic: 14.5 us -> 5.03 us
  starting transfers between devices: 16.2 us -> 7.21 us
  matrix products: 42 us -> 47 us
    reduce_scatter x0 -> x2, waiting for transfers between devices: none -> 59 us  [the longest x1 34.3 us: shards(): lax.psum_scatter(out_part.astype(jnp.bfloat16), 'etp', scatter_dimension=...]
    all_gather x0 -> x2, waiting for transfers between devices: none -> 44.7 us  [the longest x1 24.8 us: shards(): lax.all_gather(recv[:, :per_split], 'etp', axis=0, tiled=False)]
    all_to_all x3 -> x1, waiting for transfers between devices: 43.9 us -> 2.37 us  [shards(): lax.all_to_all(back, 'expert', split_axis=0, concat_axis=0, tiled=True)]
    psum x1, waiting for transfers between devices: 72.5 us -> 52.7 us  [shards(): total = lax.psum(packed, 'etp')]
    all_to_all x1, blocking collectives: 32.6 us -> 17.9 us  [shards(): lax.all_to_all(send, 'expert', split_axis=0, concat_axis=0, tiled=True)]
    gather x5 -> x0, local copies, waits for them, and re-layouts: 12.9 us -> none  [the longest x1 4.22 us: shards(): out_back.reshape(expert_count * capacity, features)[position]]
    reduce_sum x3 -> x1, other arithmetic: 10.3 us -> 0.09 us  [shards(): slots = jnp.sum(before * expert_hot, axis=1)]
    reshape x3 -> x8, local copies, waits for them, and re-layouts: 0.34 us -> 10.3 us  [the longest x1 3.94 us: shards(): lax.all_gather(recv[:, per_split:], 'etp', axis=0, tiled=False)]
  transfers between devices with their start and end apart: 4 -> 6, of which waited for: 3 -> 6; matrix products, arithmetic and copies ran while one was open for 18% -> 11% of each run, Pallas kernels for 0% -> 0%
where the time goes in v1:
time: 279 us; the launch traced here: 276 us
  waiting for transfers between devices  160 us (57%)
  matrix products  47 us (17%)
  local copies, waits for them, and re-layouts  25.6 us (9%)
  blocking collectives  17.9 us (6%)
  between operations  14 us (5%)
  starting transfers between devices  7.21 us (3%)
  other arithmetic  5.03 us (2%)
    psum x1, waiting for transfers between devices, shards(): total = lax.psum(packed, 'etp')  52.7 us
    reduce_scatter x1, waiting for transfers between devices, shards(): lax.psum_scatter(out_part.astype(jnp.bfloat16), 'etp', scatter_dimension=...  34.3 us
    all_gather x1, waiting for transfers between devices, shards(): lax.all_gather(recv[:, :per_split], 'etp', axis=0, tiled=False)  24.8 us
    reduce_scatter x1, waiting for transfers between devices, shards(): lax.psum_scatter(input_part.astype(jnp.bfloat16), 'etp', scatter_dimensio...  24.7 us
    all_gather x1, waiting for transfers between devices, shards(): lax.all_gather(recv[:, per_split:], 'etp', axis=0, tiled=False)  19.9 us
    all_to_all x1, blocking collectives, shards(): lax.all_to_all(send, 'expert', split_axis=0, concat_axis=0, tiled=True)  17.9 us
    dot_general x3, matrix products, contract_first(): lax.dot_general(left, right, (((0,), (0,)), ((), ())), preferred_element_...  14.9 us
    dot_general x3, matrix products, contract_last(): lax.dot_general(left, right, (((1,), (1,)), ((), ())), preferred_element_...  11.2 us
  transfers between devices with their start and end apart: 6, of which 6 were waited for; matrix products, arithmetic and copies ran while one was open for 11% of the time, Pallas kernels for 0%

profile of v1, /device:TPU:1, one launch (start us, length us, event | category | flops | bytes accessed | tf_op | source)
XLA Modules:
  0.0 276.2 jit_solution(1817235935620506145)
XLA Ops:
  8.3 2.1 mul.74.clone
  10.5 2.4 mul.75
  17.1 17.9 %all_to_all.10 = bf16[16,8,2048]{2,1,0:T(8,128)(2,1)S(1)} all-to-all(bf16[16,8,2048]{2,1,0:T(8,128)(2,1)S(1)} %pad_maximum_fusion), channel_id=1, replica_groups=mesh['expert'=16,'etp'=8] {'expert'}, dimensions={0} | all-to-all | bytes 1048576 | tf_op jit(solution)/shard_map/all_to_all | solution.py:78
  37.0 24.8 %all-gather.5.cloned.1.call-done = bf16[128,4,2048]{2,1,0:T(4,128)(2,1)} async-done(((bf16[16,4,2048]{2,1,0:T(4,128)(2,1)}), bf16[128,4,2048]{2,1,0:T(4,128)(2,1)}) %all-gather.5.cloned.1.call-update) | async-done | bytes 2097168 | tf_op jit(solution)/shard_map/all_gather | solution.py:79
  61.8 2.5 reshape.133
  64.3 5.6 %fusion.10 = f32[512,896]{1,0:T(8,128)} fusion(bf16[512,2048]{1,0:T(8,128)(2,1)S(1)} %reshape.133, bf16[1,2048,896]{2,1,0:T(8,128)(2,1)} %param.11), kind=kOutput, calls=%fused_computation.11 | convolution fusion | flops 1879048192 | bytes 7602176 | tf_op jit(solution)/shard_map/dot_general | solution.py:26
  69.9 19.9 %all-gather.7.cloned.1.call-done = bf16[128,4,2048]{2,1,0:T(4,128)(2,1)} async-done(((bf16[16,4,2048]{2,1,0:T(4,128)(2,1)}), bf16[128,4,2048]{2,1,0:T(4,128)(2,1)}) %all-gather.7.cloned.1.call-update) | async-done | bytes 2097168 | tf_op jit(solution)/shard_map/all_gather | solution.py:82
  89.9 3.9 %reshape.135 = bf16[512,2048]{1,0:T(8,128)(2,1)} reshape(bf16[128,4,2048]{2,1,0:T(4,128)(2,1)} %all-gather.7.cloned.1.call-done) | data formatting | bytes 4194304 | tf_op jit(solution)/shard_map/reshape | solution.py:82
  93.8 5.2 %fusion = f32[512,896]{1,0:T(8,128)S(1)} fusion(bf16[512,2048]{1,0:T(8,128)(2,1)} %reshape.135, bf16[1,896,2048]{2,1,0:T(8,128)(2,1)} %param.13), kind=kOutput, calls=%fused_computation.1 | convolution fusion | flops 1879048192 | bytes 7602176 | tf_op jit(solution)/shard_map/dot_general | solution.py:10
  99.0 3.8 %multiply_convert_fusion.3 = (bf16[512,896]{1,0:T(8,128)(2,1)}, bf16[512,896]{1,0:T(8,128)(2,1)S(1)}, bf16[512,896]{1,0:T(8,128)(2,1)S(1)}) fusion(f32[512,896]{1,0:T(8,128)S(1)} %copy-done.10, f32[512,896]{1,0:T(8,128)S(1)} %fusion, bf16[512,2048]{1,0:T(8,128)(2,1)S(1)} %reshape.133, bf16[1,2048,896]{2,1,0:T(8,128)(2,1)S(1)} %copy-done.5), kind=kOutput, calls=%fused_computation.24 | convolution fusion | flops 1885929472 | bytes 12189696 | tf_op jit(solution)/shard_map/dot_general | solution.py:27
  102.8 2.4 fusion.4
  105.5 3.7 %add_convert_fusion = bf16[512,2048]{1,0:T(8,128)(2,1)} fusion(f32[512,2048]{1,0:T(8,128)S(1)} %fusion.4, bf16[512,896]{1,0:T(8,128)(2,1)S(1)} %get-tuple-element.47, bf16[1,2048,896]{2,1,0:T(8,128)(2,1)S(1)} %copy-done.6), kind=kOutput, calls=%fused_computation | convolution fusion | flops 1881145344 | bytes 10878976 | tf_op jit(solution)/shard_map/dot_general | solution.py:10
  109.3 6.0 %fusion.12 = bf16[512,2048]{1,0:T(8,128)(2,1)} fusion(bf16[512,896]{1,0:T(8,128)(2,1)} %get-tuple-element.46, bf16[1,896,2048]{2,1,0:T(8,128)(2,1)} %param.13), kind=kOutput, calls=%fused_computation.16 | convolution fusion | flops 1880096768 | bytes 6684672 | tf_op jit(solution)/shard_map/dot_general | solution.py:31
  115.3 24.7 %reduce-scatter.5.cloned.1.call-done = bf16[64,2048]{1,0:T(8,128)(2,1)} async-done(((bf16[512,2048]{1,0:T(8,128)(2,1)}), bf16[64,2048]{1,0:T(8,128)(2,1)}) %reduce-scatter.5.cloned.1.call-update) | async-done | bytes 262160 | tf_op jit(solution)/shard_map/reduce_scatter | solution.py:90
  141.1 34.3 %reduce-scatter.3.cloned.1.call-done = bf16[64,2048]{1,0:T(8,128)(2,1)} async-done(((bf16[512,2048]{1,0:T(8,128)(2,1)}), bf16[64,2048]{1,0:T(8,128)(2,1)}) %reduce-scatter.3.cloned.1.call-update) | async-done | bytes 262160 | tf_op jit(solution)/shard_map/reduce_scatter | solution.py:89
  179.1 6.6 %all-to-all-start.1 = ((bf16[16,8,2048]{2,1,0:T(8,128)(2,1)}), bf16[16,8,2048]{2,1,0:T(8,128)(2,1)}, u32[]{:S(2)}, u32[]{:S(2)}) async-start(bf16[16,8,2048]{2,1,0:T(8,128)(2,1)} %pad_maximum_fusion.1), calls=%async_computation.3 | async-start | bytes 1048576 | tf_op jit(solution)/shard_map/all_to_all | solution.py:100
  187.1 5.4 %convert_bitcast_fusion.2 = bf16[1,2048,896]{2,1,0:T(8,128)(2,1)} fusion(bf16[512,2048]{1,0:T(8,128)(2,1)S(1)} %reshape.133, bf16[512,896]{1,0:T(8,128)(2,1)} %copy-done.9), kind=kOutput, calls=%fused_computation.15 | convolution fusion | flops 1880883200 | bytes 6684672 | tf_op jit(solution)/shard_map/dot_general | solution.py:16
  192.5 2.4 all-to-all-done.1
  197.7 2.8 %multiply_reduce_fusion = (f32[128,2]{0,1:T(2,128)S(1)}, bf16[128,2048]{1,0:T(8,128)(2,1)}) fusion(f32[128,2048]{1,0:T(8,128)} %convert_element_type.73, f32[128,2]{0,1:T(2,128)S(1)} %copy-done.4, bf16[64,2048,1]{1,0,2:T(8,128)(2,1)} %reshape.143, s32[128,2]{0,1:T(2,128)S(1)} %compare_select_fusion.1), kind=kOutput, calls=%fused_computation.19 | convolution fusion | flops 68960000 | bytes 1838080 | tf_op jit(solution)/shard_map/dot_general | solution.py:22
  200.8 2.9 %concatenate.11 = bf16[128,4224]{1,0:T(8,128)(2,1)} concatenate(bf16[128,2048]{1,0:T(8,128)(2,1)} %get-tuple-element.43, bf16[128,2048]{1,0:T(8,128)(2,1)S(1)} %convolution_reduce_fusion, bf16[128,2]{1,0:T(8,128)(2,1)S(1)} %copy.77, bf16[128,2]{1,0:T(8,128)(2,1)S(1)} %copy.78, bf16[128,124]{1,0:T(8,128)(2,1)S(1)} %broadcast_in_dim.10), dimensions={1} | concatenate | bytes 2162688 | tf_op jit(solution)/shard_map/concatenate | solution.py:114
  203.7 5.5 %convert_bitcast_fusion.1 = bf16[1,2048,896]{2,1,0:T(8,128)(2,1)} fusion(bf16[512,2048]{1,0:T(8,128)(2,1)S(1)} %reshape.133, bf16[512,896]{1,0:T(8,128)(2,1)} %copy-done.7), kind=kOutput, calls=%fused_computation.14 | convolution fusion | flops 1880883200 | bytes 6684672 | tf_op jit(solution)/shard_map/dot_general | solution.py:16
  209.2 4.0 %convert_bitcast_fusion = bf16[1,896,2048]{2,1,0:T(8,128)(2,1)} fusion(bf16[512,896]{1,0:T(8,128)(2,1)S(1)} %copy-done.8, bf16[512,2048]{1,0:T(8,128)(2,1)S(1)} %copy-done.2), kind=kOutput, calls=%fused_computation.13 | convolution fusion | flops 1880883200 | bytes 6684672 | tf_op jit(solution)/shard_map/dot_general | solution.py:16
  213.2 52.7 %all-reduce.2.cloned.1.call-done = bf16[128,4224]{1,0:T(8,128)(2,1)} async-done(((bf16[128,4224]{1,0:T(8,128)(2,1)}), bf16[128,4224]{1,0:T(8,128)(2,1)}) %all-reduce.2.cloned.1.call-update) | async-done | bytes 1081360 | tf_op jit(solution)/shard_map/psum | solution.py:124
  267.4 2.3 fusion.33
  (68 shorter events, 18.5 us)
Async XLA Ops:
  7.2 9.3 %copy-start = (bf16[128,2048]{1,0:T(8,128)(2,1)S(1)}, bf16[128,2048]{1,0:T(8,128)(2,1)}, u32[]{:S(2)}) copy-start(bf16[128,2048]{1,0:T(8,128)(2,1)} %param.7) | copy-start | bytes 1572868
  7.2 54.6 %all-gather.5.cloned.1.call-start = ((), (), s32[]{:S(2)}) async-start(), calls=%async_computation.7 | async-start | bytes 2359296 | tf_op jit(solution)/shard_map/all_gather | solution.py:79
  10.4 2.5 copy-start.4
  12.9 3.5 %copy-start.3 = (s32[128,2]{0,1:T(2,128)S(1)}, s32[128,2]{0,1:T(2,128)}, u32[]{:S(2)}) copy-start(s32[128,2]{0,1:T(2,128)} %param.9) | copy-start | bytes 3076
  36.0 53.8 %all-gather.7.cloned.1.call-start = ((), (), s32[]{:S(2)}) async-start(), calls=%async_computation.8 | async-start | bytes 2359296 | tf_op jit(solution)/shard_map/all_gather | solution.py:82
  36.8 103.2 %reduce-scatter.5.cloned.1.call-start = ((), (), s32[]{:S(2)}) async-start(), calls=%async_computation.5 | async-start | bytes 2359296 | tf_op jit(solution)/shard_map/reduce_scatter | solution.py:90
  93.8 5.2 %copy-start.5 = (bf16[1,2048,896]{2,1,0:T(8,128)(2,1)S(1)}, bf16[1,2048,896]{2,1,0:T(8,128)(2,1)}, u32[]{:S(2)}) copy-start(bf16[1,2048,896]{2,1,0:T(8,128)(2,1)} %param.12) | copy-start | bytes 11010052
  93.8 5.2 %copy-start.10 = (f32[512,896]{1,0:T(8,128)S(1)}, f32[512,896]{1,0:T(8,128)}, u32[]{:S(2)}) copy-start(f32[512,896]{1,0:T(8,128)} %fusion.10) | copy-start | bytes 5505028
  102.8 2.4 copy-start.7
  102.8 2.4 copy-start.9
  102.8 2.7 copy-start.6
  109.3 66.1 %reduce-scatter.3.cloned.1.call-start = ((), (), s32[]{:S(2)}) async-start(), calls=%async_computation.4 | async-start | bytes 2359296 | tf_op jit(solution)/shard_map/reduce_scatter | solution.py:89
  115.3 70.7 %copy-start.1 = (bf16[128,2048]{1,0:T(8,128)(2,1)S(1)}, bf16[128,2048]{1,0:T(8,128)(2,1)}, u32[]{:S(2)}) copy-start(bf16[128,2048]{1,0:T(8,128)(2,1)} %param.8) | copy-start | bytes 1572868
  179.1 15.7 %all-to-all-start.1 = ((bf16[16,8,2048]{2,1,0:T(8,128)(2,1)}), bf16[16,8,2048]{2,1,0:T(8,128)(2,1)}, u32[]{:S(2)}, u32[]{:S(2)}) async-start(bf16[16,8,2048]{2,1,0:T(8,128)(2,1)} %pad_maximum_fusion.1), calls=%async_computation.3 | async-start | bytes 1048576 | tf_op jit(solution)/shard_map/all_to_all | solution.py:100
  185.7 80.1 %all-reduce.2.cloned.1.call-start = ((), (), s32[]{:S(2)}) async-start(), calls=%async_computation.6 | async-start | bytes 2162688 | tf_op jit(solution)/shard_map/psum | solution.py:124
  203.7 5.6 %copy-start.2 = (bf16[512,2048]{1,0:T(8,128)(2,1)S(1)}, bf16[512,2048]{1,0:T(8,128)(2,1)}, u32[]{:S(2)}) copy-start(bf16[512,2048]{1,0:T(8,128)(2,1)} %reshape.135) | copy-start | bytes 6291460
  203.7 5.6 %copy-start.8 = (bf16[512,896]{1,0:T(8,128)(2,1)S(1)}, bf16[512,896]{1,0:T(8,128)(2,1)}, u32[]{:S(2)}) copy-start(bf16[512,896]{1,0:T(8,128)(2,1)} %get-tuple-element.46) | copy-start | bytes 2752516
Sparse Core Ops, SparseCore 0:
  36.1 25.5 all-gather.4
  64.1 25.7 all-gather.6
  109.4 30.5 reduce-scatter.4
  142.8 32.4 reduce-scatter.2
  203.8 62.0 all-reduce.1
